TPU v7x, 32 devices: a whole 2x2x4 slice. The times are simulated.
32 devices in a mesh: expert: 16 (over z, y, core), dp: 2 (over x).
Axes of the slice: x: 2, y: 2, z: 4, core: 2. Of those that a mesh axis runs over, the one named last changes fastest.
Arguments:
- tokens: bfloat16 [4096, 2048], P(('expert', 'dp')), may hold values from -6 to 6
- cotangent: bfloat16 [4096, 2048], P(('expert', 'dp')), may hold values from -6 to 6
- expert_ids: int32 [4096, 6], P(('expert', 'dp')), may hold values from 0 to 15, all different within a row; in each aligned block of 128 rows (0 to 127, 128 to 255, ...) at most 60 rows name the same one
- gate_vals: float32 [4096, 6], P(('expert', 'dp')), may hold values from 0.05 to 0.5
- capacity: int32 [16], replicated, may hold values from 384 to 960
- w_gate: bfloat16 [16, 384, 2048], P('expert', 'dp'), may hold values from -0.125 to 0.125
- w_up: bfloat16 [16, 384, 2048], P('expert', 'dp'), may hold values from -0.125 to 0.125
- w_down: bfloat16 [16, 384, 2048], P('expert', 'dp'), may hold values from -0.3125 to 0.3125
Outputs:
- layer_out: bfloat16 [4096, 2048], P(('expert', 'dp'))
- grad_tokens: bfloat16 [4096, 2048], P(('expert', 'dp'))
- grad_gates: float32 [4096, 6], P(('expert', 'dp'))
- grad_gate_w: bfloat16 [16, 384, 2048], P('expert', 'dp')
- grad_up_w: bfloat16 [16, 384, 2048], P('expert', 'dp')
- grad_down_w: bfloat16 [16, 384, 2048], P('expert', 'dp')
Inputs may be any that keep to these rules, and one draw needn't show every extreme that they name: `expert_ids`: within the 128 rows of one device no expert is named more than 60 times, a bound that some block reaches.
All inputs are finite; a program needn't handle non-finite values.
Results may differ from a plain program's by a relative error of at most 0.0065.
Values may be sent and summed in bfloat16 or wider, within the bound.
No kernel may reach another device: no remote copies, remote signals or barrier semaphores. Data moves between devices by JAX's collectives and lax.ppermute only.
A program may use at most 128 MiB of HBM per device.

v0:
```python
import jax
import jax.numpy as jnp
from jax import lax
from jax.sharding import PartitionSpec as P


def entering(value, axis, join, neutral):
    count, mine = (lax.axis_size(axis), lax.axis_index(axis))
    pieces = lax.all_gather(value, axis)
    subtotal = jnp.full_like(value, 0) + jnp.asarray(neutral, value.dtype)

    def lap(position, subtotal):
        longer = join(subtotal, pieces[position])
        return jnp.where(position < mine, longer, subtotal)

    return lax.fori_loop(0, count - 1, lap, subtotal)


def add_counts(earlier, later):
    return earlier + later


def on_device(tokens, cotangent, expert_ids, gate_vals, capacity, w_gate, w_up, w_down):
    tok_rows, width = tokens.shape
    top_count = expert_ids.shape[1]
    experts = capacity.shape[0]
    local_experts = w_gate.shape[0]
    slots = max(2, (5 * tok_rows * top_count + 4 * experts - 1) // (4 * experts))
    n_expert = lax.axis_size("expert")
    flat_ids = expert_ids.reshape(-1)
    one_hot = (flat_ids[:, None] == jnp.arange(experts, dtype=jnp.int32)[None, :]).astype(jnp.int32)
    running = jnp.cumsum(one_hot, axis=0)
    local_rank = jnp.sum(running * one_hot, axis=1) - 1
    counts = running[-1]
    earlier = entering(counts, "expert", add_counts, jnp.zeros_like(counts))
    offset = jnp.sum(one_hot * earlier[None, :], axis=1)
    limit = jnp.sum(one_hot * capacity[None, :], axis=1)
    kept = offset + local_rank < limit
    slot_index = jnp.where(kept, flat_ids * slots + local_rank, experts * slots)
    input_routes = jnp.broadcast_to(tokens[:, None, :], (tok_rows, top_count, width)).reshape(
        -1, width
    )
    cot_routes = (
        (gate_vals[:, :, None] * cotangent.astype(jnp.float32)[:, None, :])
        .astype(jnp.bfloat16)
        .reshape(-1, width)
    )
    input_buf = (
        jnp.zeros((experts * slots, width), jnp.bfloat16)
        .at[slot_index]
        .set(input_routes, mode="drop")
    )
    cot_buf = (
        jnp.zeros((experts * slots, width), jnp.bfloat16)
        .at[slot_index]
        .set(cot_routes, mode="drop")
    )
    input_buf = input_buf.reshape(experts, slots, width)
    cot_buf = cot_buf.reshape(experts, slots, width)
    full_gate, full_up, full_down = (
        lax.all_gather(w_gate, "dp", axis=1, tiled=True),
        lax.all_gather(w_up, "dp", axis=1, tiled=True),
        lax.all_gather(w_down, "dp", axis=1, tiled=True),
    )
    rows_in, rows_cot = (
        lax.all_to_all(input_buf, "expert", split_axis=0, concat_axis=0, tiled=True),
        lax.all_to_all(cot_buf, "expert", split_axis=0, concat_axis=0, tiled=True),
    )
    rows_in = rows_in.reshape(n_expert, local_experts, slots, width)
    gate_pre = jnp.einsum("secd,efd->secf", rows_in, full_gate, preferred_element_type=jnp.float32)
    up_pre = jnp.einsum("secd,efd->secf", rows_in, full_up, preferred_element_type=jnp.float32)
    sigmoid_gate = jax.nn.sigmoid(gate_pre)
    activated = gate_pre * sigmoid_gate
    hidden = (activated * up_pre).astype(jnp.bfloat16)
    out_rows = jnp.einsum(
        "secf,efd->secd", hidden, full_down, preferred_element_type=jnp.float32
    ).astype(jnp.bfloat16)
    rows_cot = rows_cot.reshape(n_expert, local_experts, slots, width)
    d_hidden = jnp.einsum("secd,efd->secf", rows_cot, full_down, preferred_element_type=jnp.float32)
    d_gate = (d_hidden * up_pre * (sigmoid_gate + activated * (1.0 - sigmoid_gate))).astype(
        jnp.bfloat16
    )
    d_up = (d_hidden * activated).astype(jnp.bfloat16)
    dx_rows = jnp.einsum("secf,efd->secd", d_gate, full_gate, preferred_element_type=jnp.float32)
    dx_rows = (
        dx_rows + jnp.einsum("secf,efd->secd", d_up, full_up, preferred_element_type=jnp.float32)
    ).astype(jnp.bfloat16)
    part_down = jnp.einsum("secf,secd->efd", hidden, rows_cot, preferred_element_type=jnp.float32)
    part_gate = jnp.einsum("secf,secd->efd", d_gate, rows_in, preferred_element_type=jnp.float32)
    part_up = jnp.einsum("secf,secd->efd", d_up, rows_in, preferred_element_type=jnp.float32)
    summed_gate, summed_up, summed_down = (
        lax.psum_scatter(part_gate, "dp", scatter_dimension=1, tiled=True),
        lax.psum_scatter(part_up, "dp", scatter_dimension=1, tiled=True),
        lax.psum_scatter(part_down, "dp", scatter_dimension=1, tiled=True),
    )
    grad_gate_w = summed_gate.astype(jnp.bfloat16)
    grad_up_w = summed_up.astype(jnp.bfloat16)
    grad_down_w = summed_down.astype(jnp.bfloat16)
    out_rows = out_rows.reshape(n_expert * local_experts, slots, width)
    dx_rows = dx_rows.reshape(n_expert * local_experts, slots, width)
    back_out, back_dx = (
        lax.all_to_all(out_rows, "expert", split_axis=0, concat_axis=0, tiled=True),
        lax.all_to_all(dx_rows, "expert", split_axis=0, concat_axis=0, tiled=True),
    )
    picked_out = jnp.take(
        back_out.reshape(-1, width), slot_index, axis=0, mode="fill", fill_value=0
    )
    picked_dx = jnp.take(back_dx.reshape(-1, width), slot_index, axis=0, mode="fill", fill_value=0)
    picked_out = picked_out.reshape(tok_rows, top_count, width).astype(jnp.float32)
    picked_dx = picked_dx.reshape(tok_rows, top_count, width).astype(jnp.float32)
    layer_out = jnp.sum(gate_vals[:, :, None] * picked_out, axis=1).astype(jnp.bfloat16)
    grad_tokens = jnp.sum(picked_dx, axis=1).astype(jnp.bfloat16)
    grad_gates = jnp.sum(cotangent.astype(jnp.float32)[:, None, :] * picked_out, axis=-1)
    return (layer_out, grad_tokens, grad_gates, grad_gate_w, grad_up_w, grad_down_w)


def solution(mesh):
    placed = (
        P(("expert", "dp"), None),
        P(("expert", "dp"), None),
        P(("expert", "dp"), None),
        P(("expert", "dp"), None),
        P(),
        P("expert", "dp", None),
        P("expert", "dp", None),
        P("expert", "dp", None),
    )
    return jax.shard_map(
        on_device,
        mesh=mesh,
        in_specs=placed,
        out_specs=(
            P(("expert", "dp"), None),
            P(("expert", "dp"), None),
            P(("expert", "dp"), None),
            P("expert", "dp", None),
            P("expert", "dp", None),
            P("expert", "dp", None),
        ),
        check_vma=False,
    )
```

profile of v0, /device:TPU:13, one launch (start us, length us, event | category | flops | bytes accessed | tf_op | source)
XLA Modules:
  0.0 527.0 jit_solution(4731755545639999676)
XLA Ops:
  7.2 0.7 broadcast_multiply_fusion
  7.9 0.8 copy.30
  9.2 1.7 reduce-window.6
  11.5 15.5 %all-gather = s32[16,1,16]{2,1,0:T(1,128)S(1)} all-gather(s32[1,1,16]{2,1,0:T(1,128)S(1)} %bitcast.121), channel_id=1, replica_groups=mesh['expert'=16,'dp'=2] {'expert'}, dimensions={0}, use_global_device_ids=true | all-gather | bytes 1088 | tf_op jit(solution)/shard_map/all_gather | solution.py:9
  27.6 0.8 select_reduce_fusion.2
  28.3 3.6 broadcast_in_dim.15
  32.0 4.9 reshape.202
  36.9 9.2 %scatter_custom_fusion = bf16[960,2048]{1,0:T(8,128)(2,1)} fusion(s32[768]{0:T(1024)S(1)} %fusion.27, bf16[768,2048]{1,0:T(8,128)(2,1)S(1)} %reshape.202, bf16[]{:T(256)} %constant.54.clone.1), kind=kCustom, calls=%fused_computation.19 | custom fusion | bytes 3932162 | tf_op jit(solution)/shard_map/scatter | solution.py:51
  46.1 4.9 reshape.170
  51.0 11.9 %all-to-all-start = ((bf16[16,60,2048]{2,1,0:T(8,128)(2,1)}), bf16[16,60,2048]{2,1,0:T(8,128)(2,1)}, u32[]{:S(2)}, u32[]{:S(2)}) async-start(bf16[16,60,2048]{2,1,0:T(8,128)(2,1)} %reshape.170), calls=%async_computation | async-start | bytes 8388608 | tf_op jit(solution)/shard_map/all_to_all | solution.py:66
  63.2 4.3 mul.106
  67.5 8.3 %mul.107 = f32[768,2048]{1,0:T(8,128)} reshape(f32[128,6,2048]{2,1,0:T(8,128)} %mul.106) | data formatting | bytes 12582912 | tf_op jit(solution)/shard_map/mul | solution.py:44
  75.7 14.3 %scatter_custom_fusion.1 = bf16[960,2048]{1,0:T(8,128)(2,1)} fusion(s32[768]{0:T(1024)S(1)} %fusion.27, f32[768,2048]{1,0:T(8,128)} %mul.107, f32[768]{0:T(1024)S(1)} %mul.104, bf16[]{:T(256)} %constant.54.clone.1), kind=kCustom, calls=%fused_computation.11 | custom fusion | flops 3145728 | bytes 10227714 | tf_op jit(solution)/shard_map/scatter | solution.py:56
  90.1 4.9 reshape.176
  94.9 60.3 %all-to-all-done = bf16[16,60,2048]{2,1,0:T(8,128)(2,1)} async-done(((bf16[16,60,2048]{2,1,0:T(8,128)(2,1)}), bf16[16,60,2048]{2,1,0:T(8,128)(2,1)}, u32[]{:S(2)}, u32[]{:S(2)}) %all-to-all-start) | async-done | bytes 3932192 | tf_op jit(solution)/shard_map/all_to_all | solution.py:66
  155.3 4.9 all-to-all-start.2
  160.9 0.7 all-gather.9.cloned.1.call-update
  162.6 27.8 %all-gather.7.cloned.1.call-done = bf16[1,384,2048]{2,1,0:T(8,128)(2,1)} async-done(((bf16[1,192,2048]{2,1,0:T(8,128)(2,1)}), bf16[1,384,2048]{2,1,0:T(8,128)(2,1)}) %all-gather.7.cloned.1.call-update) | async-done | bytes 1572880 | tf_op jit(solution)/shard_map/all_gather | solution.py:62
  190.3 6.2 %fusion.13 = f32[16,60,384]{2,1,0:T(8,128)} fusion(bf16[16,60,2048]{2,1,0:T(8,128)(2,1)} %all-to-all-done, bf16[1,384,2048]{2,1,0:T(8,128)(2,1)} %all-gather.7.cloned.1.call-done), kind=kOutput, calls=%fused_computation.32 | convolution fusion | flops 1509949440 | bytes 6979584 | tf_op jit(solution)/shard_map/secd,efd->secf/dot_general | solution.py:71
  196.5 22.6 %all-gather.9.cloned.1.call-done = bf16[1,384,2048]{2,1,0:T(8,128)(2,1)} async-done(((bf16[1,192,2048]{2,1,0:T(8,128)(2,1)}), bf16[1,384,2048]{2,1,0:T(8,128)(2,1)}) %all-gather.9.cloned.1.call-update) | async-done | bytes 1572880 | tf_op jit(solution)/shard_map/all_gather | solution.py:63
  219.1 33.5 %all-to-all-done.2 = bf16[16,60,2048]{2,1,0:T(8,128)(2,1)} async-done(((bf16[16,60,2048]{2,1,0:T(8,128)(2,1)}), bf16[16,60,2048]{2,1,0:T(8,128)(2,1)}, u32[]{:S(2)}, u32[]{:S(2)}) %all-to-all-start.2) | async-done | bytes 3932192 | tf_op jit(solution)/shard_map/all_to_all | solution.py:67
  252.6 6.2 %fusion.9 = f32[16,60,384]{2,1,0:T(8,128)} fusion(bf16[16,60,2048]{2,1,0:T(8,128)(2,1)} %all-to-all-done.2, bf16[1,384,2048]{2,1,0:T(8,128)(2,1)} %all-gather.9.cloned.1.call-done), kind=kOutput, calls=%fused_computation.28 | convolution fusion | flops 1509949440 | bytes 6979584 | tf_op jit(solution)/shard_map/secd,efd->secf/dot_general | solution.py:79
  258.8 6.4 %fusion.23 = (bf16[16,60,384]{2,1,0:T(8,128)(2,1)S(1)}, bf16[16,1,60,384]{3,2,0,1:T(8,128)(2,1)S(1)}, bf16[16,60,384]{2,1,0:T(8,128)(2,1)S(1)}) fusion(f32[16,60,384]{2,1,0:T(8,128)} %fusion.9, f32[16,60,384]{2,1,0:T(8,128)} %fusion.13, bf16[16,60,2048]{2,1,0:T(8,128)(2,1)} %all-to-all-done, bf16[1,384,2048]{2,1,0:T(8,128)(2,1)} %all-gather.5.cloned.1.call-done), kind=kOutput, calls=%fused_computation.44 | convolution fusion | flops 1515110400 | bytes 10665984 | tf_op jit(solution)/shard_map/secd,efd->secf/dot_general | solution.py:70
  265.2 5.7 %convolution_bitcast_fusion = f32[1,384,2048]{2,1,0:T(8,128)} fusion(bf16[16,60,384]{2,1,0:T(8,128)(2,1)S(1)} %get-tuple-element.135, bf16[16,60,2048]{2,1,0:T(8,128)(2,1)} %all-to-all-done.2), kind=kOutput, calls=%fused_computation.15 | convolution fusion | flops 1509949440 | bytes 7815168 | tf_op jit(solution)/shard_map/secf,secd->efd/dot_general | solution.py:88
  270.9 5.7 %convolution_convert_fusion = bf16[16,60,2048]{2,1,0:T(8,128)(2,1)} fusion(bf16[16,60,384]{2,1,0:T(8,128)(2,1)S(1)} %get-tuple-element.135, bf16[1,384,2048]{2,1,0:T(8,128)(2,1)} %all-gather.9.cloned.1.call-done), kind=kOutput, calls=%fused_computation.10 | convolution fusion | flops 1511915520 | bytes 6242304 | tf_op jit(solution)/shard_map/secf,efd->secd/dot_general | solution.py:75
  276.6 4.9 all-to-all-start.1
  281.8 5.6 %convolution_bitcast_fusion.2 = f32[1,384,2048]{2,1,0:T(8,128)} fusion(bf16[16,60,2048]{2,1,0:T(8,128)(2,1)} %all-to-all-done, bf16[16,1,60,384]{3,2,0,1:T(8,128)(2,1)S(1)} %get-tuple-element.134), kind=kOutput, calls=%fused_computation.17 | convolution fusion | flops 1509949440 | bytes 7815168 | tf_op jit(solution)/shard_map/secf,secd->efd/dot_general | solution.py:89
  287.5 1.5 copy-done.1
  288.9 2.3 fusion.18
  291.3 4.4 add_convert_fusion
  295.7 78.3 %all-to-all-done.1 = bf16[16,60,2048]{2,1,0:T(8,128)(2,1)} async-done(((bf16[16,60,2048]{2,1,0:T(8,128)(2,1)}), bf16[16,60,2048]{2,1,0:T(8,128)(2,1)}, u32[]{:S(2)}, u32[]{:S(2)}) %all-to-all-start.1) | async-done | bytes 3932192 | tf_op jit(solution)/shard_map/all_to_all | solution.py:102
  374.0 4.9 all-to-all-start.3
  379.0 5.7 %convolution_bitcast_fusion.1 = f32[1,384,2048]{2,1,0:T(8,128)} fusion(bf16[16,60,384]{2,1,0:T(8,128)(2,1)S(1)} %get-tuple-element.133, bf16[16,60,2048]{2,1,0:T(8,128)(2,1)} %all-to-all-done), kind=kOutput, calls=%fused_computation.16 | convolution fusion | flops 1509949440 | bytes 7815168 | tf_op jit(solution)/shard_map/secf,secd->efd/dot_general | solution.py:90
  384.7 2.4 convert_element_type.71
  387.1 2.4 convert_element_type.69
  389.5 39.2 %reduce-scatter.6.cloned.1.call-done = f32[1,192,2048]{2,1,0:T(8,128)} async-done(((f32[1,384,2048]{2,1,0:T(8,128)}), f32[1,192,2048]{2,1,0:T(8,128)}) %reduce-scatter.6.cloned.1.call-update) | async-done | bytes 1572880 | tf_op jit(solution)/shard_map/reduce_scatter | solution.py:93
  428.7 2.4 convert_element_type.70
  431.1 5.1 reshape.175
  436.3 9.0 %gather_fusion = bf16[768,2048]{1,0:T(8,128)(2,1)S(1)} fusion(bf16[960,2048]{1,0:T(8,128)(2,1)} %reshape.175, s32[1024]{0:T(1024)S(1)} %pad_clamp_fusion), kind=kCustom, calls=%fused_computation.clone | custom fusion | bytes 6294528 | tf_op jit(solution)/shard_map/jit(_take)/gather | solution.py:105
  445.2 3.8 multiply_reduce_fusion.1
  449.8 21.6 %all-to-all-done.3 = bf16[16,60,2048]{2,1,0:T(8,128)(2,1)} async-done(((bf16[16,60,2048]{2,1,0:T(8,128)(2,1)}), bf16[16,60,2048]{2,1,0:T(8,128)(2,1)}, u32[]{:S(2)}, u32[]{:S(2)}) %all-to-all-start.3) | async-done | bytes 3932192 | tf_op jit(solution)/shard_map/all_to_all | solution.py:103
  471.4 4.8 reshape.179
  476.2 9.7 %gather_fusion.1 = bf16[768,2048]{1,0:T(8,128)(2,1)} fusion(bf16[960,2048]{1,0:T(8,128)(2,1)} %reshape.179, s32[1024]{0:T(1024)S(1)} %pad_clamp_fusion), kind=kCustom, calls=%fused_computation.1.clone | custom fusion | bytes 6294528 | tf_op jit(solution)/shard_map/jit(_take)/gather | solution.py:108
  486.0 6.2 %broadcast_select_fusion.2 = (bf16[768,2048]{1,0:T(8,128)(2,1)}, f32[768,2048]{1,0:T(8,128)}) fusion(bf16[768,2048]{1,0:T(8,128)(2,1)} %gather_fusion.1, pred[768]{0:T(1024)(128)(4,1)S(1)} %get-tuple-element.131, bf16[768,2048]{1,0:T(8,128)(2,1)S(1)} %gather_fusion), kind=kLoop, calls=%fused_computation.14 | loop fusion | flops 4718592 | bytes 15729408 | tf_op jit(solution)/shard_map/jit(_take)/select_n | solution.py:108
  492.2 6.3 %reshape.180 = bf16[128,6,2048]{2,1,0:T(8,128)(2,1)} reshape(bf16[768,2048]{1,0:T(8,128)(2,1)} %get-tuple-element.136) | data formatting | bytes 6291456 | tf_op jit(solution)/shard_map/reshape | solution.py:110
  498.5 5.7 %reduce_sum.69 = bf16[128,2048]{1,0:T(8,128)(2,1)} reduce(bf16[128,6,2048]{2,1,0:T(8,128)(2,1)} %reshape.180, bf16[]{:T(256)} %constant.54.clone.1), dimensions={1}, to_apply=%region_10.12 | reduce | flops 1310720 | bytes 3670018 | tf_op jit(solution)/shard_map/reduce_sum | solution.py:112
  504.1 8.1 %reshape.181 = f32[128,6,2048]{2,1,0:T(8,128)} reshape(f32[768,2048]{1,0:T(8,128)} %get-tuple-element.137) | data formatting | bytes 12582912 | tf_op jit(solution)/shard_map/convert_element_type | solution.py:109
  512.3 7.4 %multiply_reduce_fusion = bf16[128,2048]{1,0:T(8,128)(2,1)} fusion(f32[128,6,2048]{2,1,0:T(8,128)} %reshape.181, f32[128,6]{1,0:T(8,128)S(1)} %copy.29), kind=kLoop, calls=%fused_computation.7 | loop fusion | flops 2883584 | bytes 6818816 | tf_op jit(solution)/shard_map/reduce_sum | solution.py:111
  (55 shorter events, 5.0 us)
Async XLA Ops:
  51.0 11.9 %copy-start.3 = (f32[128,6]{0,1:T(8,128)S(1)}, f32[128,6]{0,1:T(8,128)}, u32[]{:S(2)}) copy-start(f32[128,6]{0,1:T(8,128)} %param.15) | copy-start | bytes 9220
  51.0 12.1 %copy-start.2 = (bf16[128,2048]{1,0:T(8,128)(2,1)S(1)}, bf16[128,2048]{1,0:T(8,128)(2,1)}, u32[]{:S(2)}) copy-start(bf16[128,2048]{1,0:T(8,128)(2,1)} %param.13) | copy-start | bytes 1572868
  51.0 104.2 %all-to-all-start = ((bf16[16,60,2048]{2,1,0:T(8,128)(2,1)}), bf16[16,60,2048]{2,1,0:T(8,128)(2,1)}, u32[]{:S(2)}, u32[]{:S(2)}) async-start(bf16[16,60,2048]{2,1,0:T(8,128)(2,1)} %reshape.170), calls=%async_computation | async-start | bytes 8388608 | tf_op jit(solution)/shard_map/all_to_all | solution.py:66
  155.3 97.3 %all-to-all-start.2 = ((bf16[16,60,2048]{2,1,0:T(8,128)(2,1)}), bf16[16,60,2048]{2,1,0:T(8,128)(2,1)}, u32[]{:S(2)}, u32[]{:S(2)}) async-start(bf16[16,60,2048]{2,1,0:T(8,128)(2,1)} %reshape.176), calls=%async_computation.2 | async-start | bytes 8388608 | tf_op jit(solution)/shard_map/all_to_all | solution.py:67
  160.1 30.2 %all-gather.7.cloned.1.call-start = ((), (), s32[]{:S(2)}) async-start(), calls=%async_computation.8 | async-start | bytes 2359296 | tf_op jit(solution)/shard_map/all_gather | solution.py:62
  160.8 58.2 %all-gather.9.cloned.1.call-start = ((), (), s32[]{:S(2)}) async-start(), calls=%async_computation.9 | async-start | bytes 2359296 | tf_op jit(solution)/shard_map/all_gather | solution.py:63
  161.6 97.2 %all-gather.5.cloned.1.call-start = ((), (), s32[]{:S(2)}) async-start(), calls=%async_computation.7 | async-start | bytes 2359296 | tf_op jit(solution)/shard_map/all_gather | solution.py:61
  162.3 222.4 %reduce-scatter.8.cloned.1.call-start = ((), (), s32[]{:S(2)}) async-start(), calls=%async_computation.12 | async-start | bytes 4718592 | tf_op jit(solution)/shard_map/reduce_scatter | solution.py:94
  276.6 97.4 %all-to-all-start.1 = ((bf16[16,60,2048]{2,1,0:T(8,128)(2,1)}), bf16[16,60,2048]{2,1,0:T(8,128)(2,1)}, u32[]{:S(2)}, u32[]{:S(2)}) async-start(bf16[16,60,2048]{2,1,0:T(8,128)(2,1)} %convolution_convert_fusion), calls=%async_computation.1 | async-start | bytes 8388608 | tf_op jit(solution)/shard_map/all_to_all | solution.py:102
  281.6 105.6 %reduce-scatter.4.cloned.1.call-start = ((), (), s32[]{:S(2)}) async-start(), calls=%async_computation.10 | async-start | bytes 4718592 | tf_op jit(solution)/shard_map/reduce_scatter | solution.py:92
  287.4 1.5 copy-start.1
  288.9 2.3 copy-start
  374.0 97.4 %all-to-all-start.3 = ((bf16[16,60,2048]{2,1,0:T(8,128)(2,1)}), bf16[16,60,2048]{2,1,0:T(8,128)(2,1)}, u32[]{:S(2)}, u32[]{:S(2)}) async-start(bf16[16,60,2048]{2,1,0:T(8,128)(2,1)} %add_convert_fusion), calls=%async_computation.3 | async-start | bytes 8388608 | tf_op jit(solution)/shard_map/all_to_all | solution.py:103
  378.9 49.8 %reduce-scatter.6.cloned.1.call-start = ((), (), s32[]{:S(2)}) async-start(), calls=%async_computation.11 | async-start | bytes 4718592 | tf_op jit(solution)/shard_map/reduce_scatter | solution.py:93
Sparse Core Ops, SparseCore 0:
  162.5 27.7 all-gather.6
  191.8 27.2 all-gather.8
  220.6 27.1 all-gather.4
  271.0 42.8 reduce-scatter.7
  316.1 43.3 reduce-scatter.3
  384.8 43.8 reduce-scatter.5
where the time goes:
time: 535 us; the launch traced here: 527 us
  waiting for transfers between devices  285 us (53%)
  local copies, waits for them, and re-layouts  87.3 us (16%)
  matrix products  48.3 us (9%)
  other arithmetic  48.1 us (9%)
  starting transfers between devices  27.2 us (5%)
  blocking collectives  15.5 us (3%)
  between operations  14.8 us (3%)
    all_to_all x1, waiting for transfers between devices, on_device(): lax.all_to_all(out_rows, 'expert', split_axis=0, concat_axis=0, tiled=True)  78.3 us
    all_to_all x1, waiting for transfers between devices, on_device(): lax.all_to_all(input_buf, 'expert', split_axis=0, concat_axis=0, tiled=True)  60.3 us
    reduce_scatter x1, waiting for transfers between devices, on_device(): lax.psum_scatter(part_up, 'dp', scatter_dimension=1, tiled=True)  39.2 us
    all_to_all x1, waiting for transfers between devices, on_device(): lax.all_to_all(cot_buf, 'expert', split_axis=0, concat_axis=0, tiled=True)  33.5 us
    all_gather x1, waiting for transfers between devices, on_device(): lax.all_gather(w_up, 'dp', axis=1, tiled=True)  27.8 us
    all_gather x1, waiting for transfers between devices, on_device(): lax.all_gather(w_down, 'dp', axis=1, tiled=True)  22.6 us
    all_to_all x1, waiting for transfers between devices, on_device(): lax.all_to_all(dx_rows, 'expert', split_axis=0, concat_axis=0, tiled=True)  21.6 us
    all_gather x1, blocking collectives, entering(): pieces = lax.all_gather(value, axis)  15.5 us
  transfers between devices with their start and end apart: 10, of which 7 were waited for; matrix products, arithmetic and copies ran while one was open for 18% of the time, Pallas kernels for 0%

commit v1 on v0

--- a/solution.py
+++ b/solution.py
@@ -1,7 +1,42 @@
+import functools
 import jax
 import jax.numpy as jnp
 from jax import lax
 from jax.sharding import PartitionSpec as P
+
+
+def _carry_pools(u, array_dim, array_here):
+    heard, reply = (u.shape[:array_dim], u.shape[array_dim + 1 :])
+    low = jnp.moveaxis(u.reshape(*heard, array_here, -1, *reply), array_dim, 0)
+    return low
+
+
+def produce_tracks_now(array_in, in_dim):
+    array_in = jnp.moveaxis(array_in, 0, in_dim)
+    everything = array_in.shape
+    block_now = array_in.reshape(
+        *everything[:in_dim], everything[in_dim] * everything[in_dim + 1], *everything[in_dim + 2 :]
+    )
+    return block_now
+
+
+def detail_outputs(own_rows, chip_axis, load, vec):
+    m_next, d_next = (lax.axis_size(chip_axis), lax.axis_index(chip_axis))
+    piece_next = _carry_pools(own_rows, load, m_next)
+    z1 = piece_next
+    for c in range(1, m_next):
+        near, b_now = ((d_next + c) % m_next, (d_next - c) % m_next)
+        built = lax.dynamic_index_in_dim(piece_next, near, 0)
+        series = []
+        for k in range(m_next):
+            series.append((k, (k + c) % m_next))
+        outcome_arr = lax.ppermute(built, chip_axis, series)
+        z1 = lax.dynamic_update_slice_in_dim(z1, outcome_arr, b_now, axis=0)
+    part_next = produce_tracks_now(z1, vec)
+    return part_next
+
+
+supply_rounds = functools.partial(detail_outputs, chip_axis="expert", load=0, vec=0)
 
 
 def entering(value, axis, join, neutral):
@@ -100,7 +135,7 @@
     dx_rows = dx_rows.reshape(n_expert * local_experts, slots, width)
     back_out, back_dx = (
         lax.all_to_all(out_rows, "expert", split_axis=0, concat_axis=0, tiled=True),
-        lax.all_to_all(dx_rows, "expert", split_axis=0, concat_axis=0, tiled=True),
+        supply_rounds(dx_rows),
     )
     picked_out = jnp.take(
         back_out.reshape(-1, width), slot_index, axis=0, mode="fill", fill_value=0

time: 535 us -> 577 us (1.079)
  the two profiles are of different devices: /device:TPU:13 before, /device:TPU:29 now
where the time goes in v1:
time: 577 us; the launch traced here: 570 us
  waiting for transfers between devices  251 us (44%)
  local copies, waits for them, and re-layouts  103 us (18%)
  starting transfers between devices  88.9 us (15%)
  other arithmetic  48.1 us (8%)
  matrix products  46.5 us (8%)
  blocking collectives  16.8 us (3%)
  between operations  15.1 us (3%)
    ppermute x15, waiting for transfers between devices, detail_outputs(): outcome_arr = lax.ppermute(built, chip_axis, series)  107 us
    ppermute x15, starting transfers between devices, detail_outputs(): outcome_arr = lax.ppermute(built, chip_axis, series)  66.1 us
    all_to_all x1, waiting for transfers between devices, on_device(): lax.all_to_all(input_buf, 'expert', split_axis=0, concat_axis=0, tiled=True)  59.3 us
    all_to_all x1, waiting for transfers between devices, on_device(): lax.all_to_all(cot_buf, 'expert', split_axis=0, concat_axis=0, tiled=True)  32.5 us
    all_gather x1, waiting for transfers between devices, on_device(): lax.all_gather(w_up, 'dp', axis=1, tiled=True)  27.8 us
    all_gather x1, waiting for transfers between devices, on_device(): lax.all_gather(w_down, 'dp', axis=1, tiled=True)  22.6 us
    all_gather x1, blocking collectives, entering(): pieces = lax.all_gather(value, axis)  16.8 us
    scatter x1, other arithmetic, on_device(): cot_buf = jnp.zeros((experts * slots, width), jnp.bfloat16).at[slot_index...  14.3 us
  transfers between devices with their start and end apart: 24, of which 11 were waited for; matrix products, arithmetic and copies ran while one was open for 18% of the time, Pallas kernels for 0%

profile of v1, /device:TPU:29, one launch (start us, length us, event | category | flops | bytes accessed | tf_op | source)
XLA Modules:
  0.0 569.6 jit_solution(3207785282557548299)
XLA Ops:
  11.5 16.8 %all-gather = s32[16,1,16]{2,1,0:T(1,128)S(1)} all-gather(s32[1,1,16]{2,1,0:T(1,128)S(1)} %bitcast.219), channel_id=1, replica_groups=mesh['expert'=16,'dp'=2] {'expert'}, dimensions={0}, use_global_device_ids=true | all-gather | bytes 1088 | tf_op jit(solution)/shard_map/all_gather | solution.py:44
  29.6 3.7 broadcast_in_dim.15
  33.3 4.9 reshape.257
  38.2 9.2 %scatter_custom_fusion = bf16[960,2048]{1,0:T(8,128)(2,1)} fusion(s32[768]{0:T(1024)S(1)} %fusion.27, bf16[768,2048]{1,0:T(8,128)(2,1)S(1)} %reshape.257, bf16[]{:T(256)} %constant.242.clone.1), kind=kCustom, calls=%fused_computation.19 | custom fusion | bytes 3932162 | tf_op jit(solution)/shard_map/scatter | solution.py:86
  47.4 4.9 reshape.211
  52.3 10.5 %all-to-all-start = ((bf16[16,60,2048]{2,1,0:T(8,128)(2,1)}), bf16[16,60,2048]{2,1,0:T(8,128)(2,1)}, u32[]{:S(2)}, u32[]{:S(2)}) async-start(bf16[16,60,2048]{2,1,0:T(8,128)(2,1)} %reshape.211), calls=%async_computation | async-start | bytes 8388608 | tf_op jit(solution)/shard_map/all_to_all | solution.py:101
  63.0 4.3 mul.106
  67.3 8.3 %mul.107 = f32[768,2048]{1,0:T(8,128)} reshape(f32[128,6,2048]{2,1,0:T(8,128)} %mul.106) | data formatting | bytes 12582912 | tf_op jit(solution)/shard_map/mul | solution.py:79
  75.6 14.3 %scatter_custom_fusion.1 = bf16[960,2048]{1,0:T(8,128)(2,1)} fusion(s32[768]{0:T(1024)S(1)} %fusion.27, f32[768,2048]{1,0:T(8,128)} %mul.107, f32[768]{0:T(1024)S(1)} %mul.104, bf16[]{:T(256)} %constant.242.clone.1), kind=kCustom, calls=%fused_computation.11 | custom fusion | flops 3145728 | bytes 10227714 | tf_op jit(solution)/shard_map/scatter | solution.py:91
  89.9 4.9 reshape.217
  94.8 59.3 %all-to-all-done = bf16[16,60,2048]{2,1,0:T(8,128)(2,1)} async-done(((bf16[16,60,2048]{2,1,0:T(8,128)(2,1)}), bf16[16,60,2048]{2,1,0:T(8,128)(2,1)}, u32[]{:S(2)}, u32[]{:S(2)}) %all-to-all-start) | async-done | bytes 3932192 | tf_op jit(solution)/shard_map/all_to_all | solution.py:101
  154.0 5.9 %all-to-all-start.2 = ((bf16[16,60,2048]{2,1,0:T(8,128)(2,1)}), bf16[16,60,2048]{2,1,0:T(8,128)(2,1)}, u32[]{:S(2)}, u32[]{:S(2)}) async-start(bf16[16,60,2048]{2,1,0:T(8,128)(2,1)} %reshape.217), calls=%async_computation.2 | async-start | bytes 8388608 | tf_op jit(solution)/shard_map/all_to_all | solution.py:102
  162.3 27.8 %all-gather.7.cloned.1.call-done = bf16[1,384,2048]{2,1,0:T(8,128)(2,1)} async-done(((bf16[1,192,2048]{2,1,0:T(8,128)(2,1)}), bf16[1,384,2048]{2,1,0:T(8,128)(2,1)}) %all-gather.7.cloned.1.call-update) | async-done | bytes 1572880 | tf_op jit(solution)/shard_map/all_gather | solution.py:97
  190.1 6.2 %fusion.13 = f32[16,60,384]{2,1,0:T(8,128)} fusion(bf16[16,60,2048]{2,1,0:T(8,128)(2,1)} %all-to-all-done, bf16[1,384,2048]{2,1,0:T(8,128)(2,1)} %all-gather.7.cloned.1.call-done), kind=kOutput, calls=%fused_computation.32 | convolution fusion | flops 1509949440 | bytes 6979584 | tf_op jit(solution)/shard_map/secd,efd->secf/dot_general | solution.py:106
  196.4 22.6 %all-gather.9.cloned.1.call-done = bf16[1,384,2048]{2,1,0:T(8,128)(2,1)} async-done(((bf16[1,192,2048]{2,1,0:T(8,128)(2,1)}), bf16[1,384,2048]{2,1,0:T(8,128)(2,1)}) %all-gather.9.cloned.1.call-update) | async-done | bytes 1572880 | tf_op jit(solution)/shard_map/all_gather | solution.py:98
  218.9 32.5 %all-to-all-done.2 = bf16[16,60,2048]{2,1,0:T(8,128)(2,1)} async-done(((bf16[16,60,2048]{2,1,0:T(8,128)(2,1)}), bf16[16,60,2048]{2,1,0:T(8,128)(2,1)}, u32[]{:S(2)}, u32[]{:S(2)}) %all-to-all-start.2) | async-done | bytes 3932192 | tf_op jit(solution)/shard_map/all_to_all | solution.py:102
  251.4 6.2 %fusion.9 = f32[16,60,384]{2,1,0:T(8,128)} fusion(bf16[16,60,2048]{2,1,0:T(8,128)(2,1)} %all-to-all-done.2, bf16[1,384,2048]{2,1,0:T(8,128)(2,1)} %all-gather.9.cloned.1.call-done), kind=kOutput, calls=%fused_computation.28 | convolution fusion | flops 1509949440 | bytes 6979584 | tf_op jit(solution)/shard_map/secd,efd->secf/dot_general | solution.py:114
  257.6 6.4 %fusion.23 = (bf16[16,60,384]{2,1,0:T(8,128)(2,1)S(1)}, bf16[16,1,60,384]{3,2,0,1:T(8,128)(2,1)S(1)}, bf16[16,60,384]{2,1,0:T(8,128)(2,1)S(1)}) fusion(f32[16,60,384]{2,1,0:T(8,128)} %fusion.9, f32[16,60,384]{2,1,0:T(8,128)} %fusion.13, bf16[16,60,2048]{2,1,0:T(8,128)(2,1)} %all-to-all-done, bf16[1,384,2048]{2,1,0:T(8,128)(2,1)} %all-gather.5.cloned.1.call-done), kind=kOutput, calls=%fused_computation.44 | convolution fusion | flops 1515110400 | bytes 10665984 | tf_op jit(solution)/shard_map/secd,efd->secf/dot_general | solution.py:105
  264.1 5.7 %convolution_bitcast_fusion = f32[1,384,2048]{2,1,0:T(8,128)} fusion(bf16[16,60,384]{2,1,0:T(8,128)(2,1)S(1)} %get-tuple-element.150, bf16[16,60,2048]{2,1,0:T(8,128)(2,1)} %all-to-all-done.2), kind=kOutput, calls=%fused_computation.15 | convolution fusion | flops 1509949440 | bytes 7815168 | tf_op jit(solution)/shard_map/secf,secd->efd/dot_general | solution.py:123
  269.8 5.6 convolution_bitcast_fusion.2
  275.5 5.7 %convolution_convert_fusion = bf16[16,60,2048]{2,1,0:T(8,128)(2,1)} fusion(bf16[16,60,384]{2,1,0:T(8,128)(2,1)S(1)} %get-tuple-element.150, bf16[1,384,2048]{2,1,0:T(8,128)(2,1)} %all-gather.9.cloned.1.call-done), kind=kOutput, calls=%fused_computation.10 | convolution fusion | flops 1511915520 | bytes 6242304 | tf_op jit(solution)/shard_map/secf,efd->secd/dot_general | solution.py:110
  281.2 5.9 %all-to-all-start.1 = ((bf16[16,60,2048]{2,1,0:T(8,128)(2,1)}), bf16[16,60,2048]{2,1,0:T(8,128)(2,1)}, u32[]{:S(2)}, u32[]{:S(2)}) async-start(bf16[16,60,2048]{2,1,0:T(8,128)(2,1)} %convolution_convert_fusion), calls=%async_computation.1 | async-start | bytes 8388608 | tf_op jit(solution)/shard_map/all_to_all | solution.py:137
  287.3 5.8 %convolution_bitcast_fusion.1 = f32[1,384,2048]{2,1,0:T(8,128)} fusion(bf16[16,60,384]{2,1,0:T(8,128)(2,1)S(1)} %get-tuple-element.148, bf16[16,60,2048]{2,1,0:T(8,128)(2,1)} %all-to-all-done), kind=kOutput, calls=%fused_computation.16 | convolution fusion | flops 1509949440 | bytes 7815168 | tf_op jit(solution)/shard_map/secf,secd->efd/dot_general | solution.py:125
  304.7 2.6 collective-permute-start.12
  307.3 53.5 %collective-permute-done = bf16[1,1,60,2048]{3,2,0,1:T(8,128)(2,1)} collective-permute-done((bf16[1,1,60,2048]{3,2,0,1:T(8,128)(2,1)}, bf16[1,1,60,2048]{3,2,0,1:T(8,128)(2,1)}, u32[]{:S(2)}, u32[]{:S(2)}) %collective-permute-start) | collective-permute-done | bytes 245792 | tf_op jit(solution)/shard_map/ppermute | solution.py:33
  362.4 4.0 collective-permute-done.1
  369.4 2.5 collective-permute-done.2
  371.9 25.2 %collective-permute-start.4 = (bf16[1,1,60,2048]{3,2,0,1:T(8,128)(2,1)S(1)}, bf16[1,1,60,2048]{3,2,0,1:T(8,128)(2,1)S(1)}, u32[]{:S(2)}, u32[]{:S(2)}) collective-permute-start(bf16[1,1,60,2048]{3,2,0,1:T(8,128)(2,1)S(1)} %get-tuple-element.143), channel_id=1, source_target_pairs={{0,10},{2,12},{4,14},{6,16},{8,18},{10,20},{12,22},{14,24},{16,26}... | collective-permute-start | bytes 737288 | tf_op jit(solution)/shard_map/ppermute | solution.py:33
  397.8 5.2 collective-permute-start.5
  403.7 14.2 %collective-permute-start.6 = (bf16[1,1,60,2048]{3,2,0,1:T(8,128)(2,1)S(1)}, bf16[1,1,60,2048]{3,2,0,1:T(8,128)(2,1)S(1)}, u32[]{:S(2)}, u32[]{:S(2)}) collective-permute-start(bf16[1,1,60,2048]{3,2,0,1:T(8,128)(2,1)S(1)} %get-tuple-element.141), channel_id=1, source_target_pairs={{0,14},{2,16},{4,18},{6,20},{8,22},{10,24},{12,26},{14,28},{16,30}... | collective-permute-start | bytes 737288 | tf_op jit(solution)/shard_map/ppermute | solution.py:33
  418.7 9.4 %collective-permute-start.7 = (bf16[1,1,60,2048]{3,2,0,1:T(8,128)(2,1)S(1)}, bf16[1,1,60,2048]{3,2,0,1:T(8,128)(2,1)S(1)}, u32[]{:S(2)}, u32[]{:S(2)}) collective-permute-start(bf16[1,1,60,2048]{3,2,0,1:T(8,128)(2,1)S(1)} %get-tuple-element.140), channel_id=1, source_target_pairs={{0,16},{2,18},{4,20},{6,22},{8,24},{10,26},{12,28},{14,30},{16,0},... | collective-permute-start | bytes 737288 | tf_op jit(solution)/shard_map/ppermute | solution.py:33
  428.8 5.6 collective-permute-start.8
  435.2 15.9 %collective-permute-done.7 = bf16[1,1,60,2048]{3,2,0,1:T(8,128)(2,1)S(1)} collective-permute-done((bf16[1,1,60,2048]{3,2,0,1:T(8,128)(2,1)S(1)}, bf16[1,1,60,2048]{3,2,0,1:T(8,128)(2,1)S(1)}, u32[]{:S(2)}, u32[]{:S(2)}) %collective-permute-start.7) | collective-permute-done | bytes 245792 | tf_op jit(solution)/shard_map/ppermute | solution.py:33
  452.5 24.5 %collective-permute-done.9 = bf16[1,1,60,2048]{3,2,0,1:T(8,128)(2,1)S(1)} collective-permute-done((bf16[1,1,60,2048]{3,2,0,1:T(8,128)(2,1)S(1)}, bf16[1,1,60,2048]{3,2,0,1:T(8,128)(2,1)S(1)}, u32[]{:S(2)}, u32[]{:S(2)}) %collective-permute-start.9) | collective-permute-done | bytes 245792 | tf_op jit(solution)/shard_map/ppermute | solution.py:33
  479.3 6.2 %collective-permute-done.11 = bf16[1,1,60,2048]{3,2,0,1:T(8,128)(2,1)S(1)} collective-permute-done((bf16[1,1,60,2048]{3,2,0,1:T(8,128)(2,1)S(1)}, bf16[1,1,60,2048]{3,2,0,1:T(8,128)(2,1)S(1)}, u32[]{:S(2)}, u32[]{:S(2)}) %collective-permute-start.11) | collective-permute-done | bytes 245792 | tf_op jit(solution)/shard_map/ppermute | solution.py:33
  488.4 4.9 reshape_reshape.3
  493.3 9.7 %gather_fusion.1 = bf16[768,2048]{1,0:T(8,128)(2,1)} fusion(bf16[960,2048]{1,0:T(8,128)(2,1)} %reshape_reshape.3, s32[1024]{0:T(1024)S(1)} %pad_clamp_fusion), kind=kCustom, calls=%fused_computation.1.clone | custom fusion | bytes 6294528 | tf_op jit(solution)/shard_map/jit(_take)/gather | solution.py:143
  503.0 2.4 convert_element_type.80
  505.4 2.4 convert_element_type.78
  507.8 2.4 convert_element_type.79
  510.2 4.9 reshape.216
  515.0 9.0 %gather_fusion = bf16[768,2048]{1,0:T(8,128)(2,1)S(1)} fusion(bf16[960,2048]{1,0:T(8,128)(2,1)} %reshape.216, s32[1024]{0:T(1024)S(1)} %pad_clamp_fusion), kind=kCustom, calls=%fused_computation.clone | custom fusion | bytes 6294528 | tf_op jit(solution)/shard_map/jit(_take)/gather | solution.py:140
  524.0 3.8 multiply_reduce_fusion.1
  528.6 6.2 %broadcast_select_fusion.2 = (bf16[768,2048]{1,0:T(8,128)(2,1)}, f32[768,2048]{1,0:T(8,128)}) fusion(bf16[768,2048]{1,0:T(8,128)(2,1)} %gather_fusion.1, pred[768]{0:T(1024)(128)(4,1)S(1)} %get-tuple-element.131, bf16[768,2048]{1,0:T(8,128)(2,1)S(1)} %gather_fusion), kind=kLoop, calls=%fused_computation.14 | loop fusion | flops 4718592 | bytes 15729408 | tf_op jit(solution)/shard_map/jit(_take)/select_n | solution.py:143
  534.8 6.2 %reshape.235 = bf16[128,6,2048]{2,1,0:T(8,128)(2,1)} reshape(bf16[768,2048]{1,0:T(8,128)(2,1)} %get-tuple-element.151) | data formatting | bytes 6291456 | tf_op jit(solution)/shard_map/reshape | solution.py:145
  541.0 5.7 reduce_sum.69
  546.7 8.1 %reshape.236 = f32[128,6,2048]{2,1,0:T(8,128)} reshape(f32[768,2048]{1,0:T(8,128)} %get-tuple-element.152) | data formatting | bytes 12582912 | tf_op jit(solution)/shard_map/convert_element_type | solution.py:144
  554.8 7.4 %multiply_reduce_fusion = bf16[128,2048]{1,0:T(8,128)(2,1)} fusion(f32[128,6,2048]{2,1,0:T(8,128)} %reshape.236, f32[128,6]{1,0:T(8,128)S(1)} %copy.29), kind=kLoop, calls=%fused_computation.7 | loop fusion | flops 2883584 | bytes 6818816 | tf_op jit(solution)/shard_map/reduce_sum | solution.py:146
  (101 shorter events, 35.8 us)
Async XLA Ops:
  52.3 10.5 %copy-start.4 = (f32[128,6]{0,1:T(8,128)S(1)}, f32[128,6]{0,1:T(8,128)}, u32[]{:S(2)}) copy-start(f32[128,6]{0,1:T(8,128)} %param.15) | copy-start | bytes 9220
  52.3 10.7 %copy-start.3 = (bf16[128,2048]{1,0:T(8,128)(2,1)S(1)}, bf16[128,2048]{1,0:T(8,128)(2,1)}, u32[]{:S(2)}) copy-start(bf16[128,2048]{1,0:T(8,128)(2,1)} %param.13) | copy-start | bytes 1572868
  52.3 101.7 %all-to-all-start = ((bf16[16,60,2048]{2,1,0:T(8,128)(2,1)}), bf16[16,60,2048]{2,1,0:T(8,128)(2,1)}, u32[]{:S(2)}, u32[]{:S(2)}) async-start(bf16[16,60,2048]{2,1,0:T(8,128)(2,1)} %reshape.211), calls=%async_computation | async-start | bytes 8388608 | tf_op jit(solution)/shard_map/all_to_all | solution.py:101
  154.0 97.4 %all-to-all-start.2 = ((bf16[16,60,2048]{2,1,0:T(8,128)(2,1)}), bf16[16,60,2048]{2,1,0:T(8,128)(2,1)}, u32[]{:S(2)}, u32[]{:S(2)}) async-start(bf16[16,60,2048]{2,1,0:T(8,128)(2,1)} %reshape.217), calls=%async_computation.2 | async-start | bytes 8388608 | tf_op jit(solution)/shard_map/all_to_all | solution.py:102
  159.9 30.2 %all-gather.7.cloned.1.call-start = ((), (), s32[]{:S(2)}) async-start(), calls=%async_computation.7 | async-start | bytes 2359296 | tf_op jit(solution)/shard_map/all_gather | solution.py:97
  160.6 58.3 %all-gather.9.cloned.1.call-start = ((), (), s32[]{:S(2)}) async-start(), calls=%async_computation.8 | async-start | bytes 2359296 | tf_op jit(solution)/shard_map/all_gather | solution.py:98
  161.4 96.2 %all-gather.5.cloned.1.call-start = ((), (), s32[]{:S(2)}) async-start(), calls=%async_computation.6 | async-start | bytes 2359296 | tf_op jit(solution)/shard_map/all_gather | solution.py:96
  162.1 340.9 %reduce-scatter.8.cloned.1.call-start = ((), (), s32[]{:S(2)}) async-start(), calls=%async_computation.11 | async-start | bytes 4718592 | tf_op jit(solution)/shard_map/reduce_scatter | solution.py:129
  269.8 235.6 %reduce-scatter.4.cloned.1.call-start = ((), (), s32[]{:S(2)}) async-start(), calls=%async_computation.9 | async-start | bytes 4718592 | tf_op jit(solution)/shard_map/reduce_scatter | solution.py:127
  281.2 229.0 %all-to-all-start.1 = ((bf16[16,60,2048]{2,1,0:T(8,128)(2,1)}), bf16[16,60,2048]{2,1,0:T(8,128)(2,1)}, u32[]{:S(2)}, u32[]{:S(2)}) async-start(bf16[16,60,2048]{2,1,0:T(8,128)(2,1)} %convolution_convert_fusion), calls=%async_computation.1 | async-start | bytes 8388608 | tf_op jit(solution)/shard_map/all_to_all | solution.py:137
  287.1 220.7 %reduce-scatter.6.cloned.1.call-start = ((), (), s32[]{:S(2)}) async-start(), calls=%async_computation.10 | async-start | bytes 4718592 | tf_op jit(solution)/shard_map/reduce_scatter | solution.py:128
  293.2 1.4 copy-start.2
  294.6 2.3 copy-start.1
  299.3 2.0 copy-start
  302.3 58.4 %collective-permute-start = (bf16[1,1,60,2048]{3,2,0,1:T(8,128)(2,1)}, bf16[1,1,60,2048]{3,2,0,1:T(8,128)(2,1)}, u32[]{:S(2)}, u32[]{:S(2)}) collective-permute-start(bf16[1,1,60,2048]{3,2,0,1:T(8,128)(2,1)} %get-tuple-element.147), channel_id=1, source_target_pairs={{0,2},{2,4},{4,6},{6,8},{8,10},{10,12},{12,14},{14,16},{16,18},{18... | collective-permute-start | bytes 737288 | tf_op jit(solution)/shard_map/ppermute | solution.py:33
  302.4 64.0 %collective-permute-start.1 = (bf16[1,1,60,2048]{3,2,0,1:T(8,128)(2,1)}, bf16[1,1,60,2048]{3,2,0,1:T(8,128)(2,1)}, u32[]{:S(2)}, u32[]{:S(2)}) collective-permute-start(bf16[1,1,60,2048]{3,2,0,1:T(8,128)(2,1)} %get-tuple-element.146), channel_id=1, source_target_pairs={{0,4},{2,6},{4,8},{6,10},{8,12},{10,14},{12,16},{14,18},{16,20},{1... | collective-permute-start | bytes 737288 | tf_op jit(solution)/shard_map/ppermute | solution.py:33
  304.1 183.5 %collective-permute-start.14 = (bf16[1,1,60,2048]{3,2,0,1:T(8,128)(2,1)S(1)}, bf16[1,1,60,2048]{3,2,0,1:T(8,128)(2,1)S(1)}, u32[]{:S(2)}, u32[]{:S(2)}) collective-permute-start(bf16[1,1,60,2048]{3,2,0,1:T(8,128)(2,1)S(1)} %get-tuple-element.133), channel_id=1, source_target_pairs={{0,30},{2,0},{4,2},{6,4},{8,6},{10,8},{12,10},{14,12},{16,14},{18,... | collective-permute-start | bytes 737288 | tf_op jit(solution)/shard_map/ppermute | solution.py:33
  304.1 182.8 %collective-permute-start.13 = (bf16[1,1,60,2048]{3,2,0,1:T(8,128)(2,1)S(1)}, bf16[1,1,60,2048]{3,2,0,1:T(8,128)(2,1)S(1)}, u32[]{:S(2)}, u32[]{:S(2)}) collective-permute-start(bf16[1,1,60,2048]{3,2,0,1:T(8,128)(2,1)S(1)} %get-tuple-element.134), channel_id=1, source_target_pairs={{0,28},{2,30},{4,0},{6,2},{8,4},{10,6},{12,8},{14,10},{16,12},{18,... | collective-permute-start | bytes 737288 | tf_op jit(solution)/shard_map/ppermute | solution.py:33
  304.7 181.5 %collective-permute-start.12 = (bf16[1,1,60,2048]{3,2,0,1:T(8,128)(2,1)S(1)}, bf16[1,1,60,2048]{3,2,0,1:T(8,128)(2,1)S(1)}, u32[]{:S(2)}, u32[]{:S(2)}) collective-permute-start(bf16[1,1,60,2048]{3,2,0,1:T(8,128)(2,1)S(1)} %get-tuple-element.135), channel_id=1, source_target_pairs={{0,26},{2,28},{4,30},{6,0},{8,2},{10,4},{12,6},{14,8},{16,10},{18,... | collective-permute-start | bytes 737288 | tf_op jit(solution)/shard_map/ppermute | solution.py:33
  360.8 11.1 %collective-permute-start.2 = (bf16[1,1,60,2048]{3,2,0,1:T(8,128)(2,1)S(1)}, bf16[1,1,60,2048]{3,2,0,1:T(8,128)(2,1)S(1)}, u32[]{:S(2)}, u32[]{:S(2)}) collective-permute-start(bf16[1,1,60,2048]{3,2,0,1:T(8,128)(2,1)S(1)} %get-tuple-element.145), channel_id=1, source_target_pairs={{0,6},{2,8},{4,10},{6,12},{8,14},{10,16},{12,18},{14,20},{16,22},{... | collective-permute-start | bytes 737288 | tf_op jit(solution)/shard_map/ppermute | solution.py:33
  366.4 31.5 %collective-permute-start.3 = (bf16[1,1,60,2048]{3,2,0,1:T(8,128)(2,1)S(1)}, bf16[1,1,60,2048]{3,2,0,1:T(8,128)(2,1)S(1)}, u32[]{:S(2)}, u32[]{:S(2)}) collective-permute-start(bf16[1,1,60,2048]{3,2,0,1:T(8,128)(2,1)S(1)} %get-tuple-element.144), channel_id=1, source_target_pairs={{0,8},{2,10},{4,12},{6,14},{8,16},{10,18},{12,20},{14,22},{16,24},... | collective-permute-start | bytes 737288 | tf_op jit(solution)/shard_map/ppermute | solution.py:33
  371.9 31.8 %collective-permute-start.4 = (bf16[1,1,60,2048]{3,2,0,1:T(8,128)(2,1)S(1)}, bf16[1,1,60,2048]{3,2,0,1:T(8,128)(2,1)S(1)}, u32[]{:S(2)}, u32[]{:S(2)}) collective-permute-start(bf16[1,1,60,2048]{3,2,0,1:T(8,128)(2,1)S(1)} %get-tuple-element.143), channel_id=1, source_target_pairs={{0,10},{2,12},{4,14},{6,16},{8,18},{10,20},{12,22},{14,24},{16,26}... | collective-permute-start | bytes 737288 | tf_op jit(solution)/shard_map/ppermute | solution.py:33
  397.8 20.8 %collective-permute-start.5 = (bf16[1,1,60,2048]{3,2,0,1:T(8,128)(2,1)S(1)}, bf16[1,1,60,2048]{3,2,0,1:T(8,128)(2,1)S(1)}, u32[]{:S(2)}, u32[]{:S(2)}) collective-permute-start(bf16[1,1,60,2048]{3,2,0,1:T(8,128)(2,1)S(1)} %get-tuple-element.142), channel_id=1, source_target_pairs={{0,12},{2,14},{4,16},{6,18},{8,20},{10,22},{12,24},{14,26},{16,28}... | collective-permute-start | bytes 737288 | tf_op jit(solution)/shard_map/ppermute | solution.py:33
  403.7 25.1 %collective-permute-start.6 = (bf16[1,1,60,2048]{3,2,0,1:T(8,128)(2,1)S(1)}, bf16[1,1,60,2048]{3,2,0,1:T(8,128)(2,1)S(1)}, u32[]{:S(2)}, u32[]{:S(2)}) collective-permute-start(bf16[1,1,60,2048]{3,2,0,1:T(8,128)(2,1)S(1)} %get-tuple-element.141), channel_id=1, source_target_pairs={{0,14},{2,16},{4,18},{6,20},{8,22},{10,24},{12,26},{14,28},{16,30}... | collective-permute-start | bytes 737288 | tf_op jit(solution)/shard_map/ppermute | solution.py:33
  418.7 32.3 %collective-permute-start.7 = (bf16[1,1,60,2048]{3,2,0,1:T(8,128)(2,1)S(1)}, bf16[1,1,60,2048]{3,2,0,1:T(8,128)(2,1)S(1)}, u32[]{:S(2)}, u32[]{:S(2)}) collective-permute-start(bf16[1,1,60,2048]{3,2,0,1:T(8,128)(2,1)S(1)} %get-tuple-element.140), channel_id=1, source_target_pairs={{0,16},{2,18},{4,20},{6,22},{8,24},{10,26},{12,28},{14,30},{16,0},... | collective-permute-start | bytes 737288 | tf_op jit(solution)/shard_map/ppermute | solution.py:33
  428.8 22.9 %collective-permute-start.8 = (bf16[1,1,60,2048]{3,2,0,1:T(8,128)(2,1)S(1)}, bf16[1,1,60,2048]{3,2,0,1:T(8,128)(2,1)S(1)}, u32[]{:S(2)}, u32[]{:S(2)}) collective-permute-start(bf16[1,1,60,2048]{3,2,0,1:T(8,128)(2,1)S(1)} %get-tuple-element.139), channel_id=1, source_target_pairs={{0,18},{2,20},{4,22},{6,24},{8,26},{10,28},{12,30},{14,0},{16,2},{... | collective-permute-start | bytes 737288 | tf_op jit(solution)/shard_map/ppermute | solution.py:33
  451.0 26.0 %collective-permute-start.9 = (bf16[1,1,60,2048]{3,2,0,1:T(8,128)(2,1)S(1)}, bf16[1,1,60,2048]{3,2,0,1:T(8,128)(2,1)S(1)}, u32[]{:S(2)}, u32[]{:S(2)}) collective-permute-start(bf16[1,1,60,2048]{3,2,0,1:T(8,128)(2,1)S(1)} %get-tuple-element.138), channel_id=1, source_target_pairs={{0,20},{2,22},{4,24},{6,26},{8,28},{10,30},{12,0},{14,2},{16,4},{1... | collective-permute-start | bytes 737288 | tf_op jit(solution)/shard_map/ppermute | solution.py:33
  451.8 26.8 %collective-permute-start.10 = (bf16[1,1,60,2048]{3,2,0,1:T(8,128)(2,1)S(1)}, bf16[1,1,60,2048]{3,2,0,1:T(8,128)(2,1)S(1)}, u32[]{:S(2)}, u32[]{:S(2)}) collective-permute-start(bf16[1,1,60,2048]{3,2,0,1:T(8,128)(2,1)S(1)} %get-tuple-element.137), channel_id=1, source_target_pairs={{0,22},{2,24},{4,26},{6,28},{8,30},{10,0},{12,2},{14,4},{16,6},{18... | collective-permute-start | bytes 737288 | tf_op jit(solution)/shard_map/ppermute | solution.py:33
  477.0 8.5 %collective-permute-start.11 = (bf16[1,1,60,2048]{3,2,0,1:T(8,128)(2,1)S(1)}, bf16[1,1,60,2048]{3,2,0,1:T(8,128)(2,1)S(1)}, u32[]{:S(2)}, u32[]{:S(2)}) collective-permute-start(bf16[1,1,60,2048]{3,2,0,1:T(8,128)(2,1)S(1)} %get-tuple-element.136), channel_id=1, source_target_pairs={{0,24},{2,26},{4,28},{6,30},{8,0},{10,2},{12,4},{14,6},{16,8},{18,... | collective-permute-start | bytes 737288 | tf_op jit(solution)/shard_map/ppermute | solution.py:33
Sparse Core Ops, SparseCore 0:
  162.3 27.8 all-gather.6
  191.7 27.2 all-gather.8
  220.5 27.1 all-gather.4
  269.9 43.7 reduce-scatter.7
  315.9 43.3 reduce-scatter.3
  361.4 43.3 reduce-scatter.5
